TPU v7x, 256 devices: a whole 4x4x8 slice. The times are simulated.
256 devices in a mesh: batch: 16 (over x_hi, z), dom: 16 (over x_lo, y, core).
Axes of the slice: x: 4 (x_hi: 2, x_lo: 2; x = x_hi * 2 + x_lo), y: 4, z: 8, core: 2. Of those that a mesh axis runs over, the one named last changes fastest.
Arguments:
- inputs: bfloat16 [32, 64, 68, 256], P('batch', 'dom'), may hold values from -70 to 70
- saved_q: bfloat16 [32, 64, 68, 256], P('batch', 'dom'), may hold values from -6.5 to 6.5
- saved_k: bfloat16 [32, 64, 68, 256], P('batch', 'dom'), may hold values from -6.5 to 6.5
- saved_v: bfloat16 [32, 64, 68, 256], P('batch', 'dom'), may hold values from -6 to 6
- attended: bfloat16 [32, 64, 68, 256], P('batch', 'dom'), may hold values from -6 to 6
- out_cot: bfloat16 [32, 64, 68, 256], P('batch', 'dom'), may hold values from -6 to 6
- conv_weight: bfloat16 [9, 256, 256], replicated, may hold values from -0.125 to 0.125
- qkv_weight: bfloat16 [256, 768], replicated, may hold values from -0.375 to 0.375
- out_weight: bfloat16 [256, 256], replicated, may hold values from -0.375 to 0.375
- norm_gain: float32 [256], replicated, may hold values from 0.5 to 1.5
- norm_shift: float32 [256], replicated, may hold values from -2.5 to 2.5
Outputs:
- input_grad: bfloat16 [32, 64, 68, 256], P('batch', 'dom')
- conv_grad: float32 [9, 256, 256], replicated
- qkv_grad: float32 [256, 768], replicated
- out_grad: float32 [256, 256], replicated
- gain_grad: float32 [256], replicated
- shift_grad: float32 [256], replicated
All inputs are finite; a program needn't handle non-finite values.
Results may differ from a plain program's by a relative error of at most 0.011.
Values may be sent and summed in bfloat16 or wider, within the bound.
No kernel may reach another device: no remote copies, remote signals or barrier semaphores. Data moves between devices by JAX's collectives and lax.ppermute only.
A program may use at most 128 MiB of HBM per device.

v0:
```python
import jax
import jax.numpy as jnp
from jax import lax
from jax.sharding import PartitionSpec as P

HEADS = 1
GROUPS = 32
EPSILON = 1e-05


def with_halo(cells, sides, width):
    for axis, dim in sides:
        count = lax.axis_size(axis)
        ends = count - 1
        head = lax.slice_in_dim(cells, 0, width, axis=dim)
        tail = lax.slice_in_dim(cells, cells.shape[dim] - width, cells.shape[dim], axis=dim)
        cells = jnp.concatenate(
            [
                lax.ppermute(tail, axis, [(i, (i + 1) % count) for i in range(ends)]),
                cells,
                lax.ppermute(head, axis, [((i + 1) % count, i) for i in range(ends)]),
            ],
            axis=dim,
        )
    return cells


def per_channel(values, group_width):
    return jnp.repeat(values, group_width, axis=-1)[:, None, None, :]


def body(
    inputs,
    saved_q,
    saved_k,
    saved_v,
    attended,
    out_cot,
    conv_weight,
    qkv_weight,
    out_weight,
    norm_gain,
    norm_shift,
):
    samples, row_count, col_count, chan_count = inputs.shape
    tok_count = row_count * col_count
    group_width = chan_count // GROUPS
    head_width = chan_count // HEADS
    score_scale = head_width ** (-0.5)
    count = row_count * col_count * group_width * lax.axis_size("dom")
    f32 = jnp.float32
    bf16 = jnp.bfloat16
    input_wide = inputs.astype(f32)
    grouped = input_wide.reshape(samples, row_count, col_count, GROUPS, group_width)
    group_sums = lax.psum((grouped.sum((1, 2, 4)), (grouped * grouped).sum((1, 2, 4))), "dom")
    group_mean = group_sums[0] / count
    group_var = group_sums[1] / count - group_mean * group_mean
    inv_std = lax.rsqrt(group_var + EPSILON)
    normed = (input_wide - per_channel(group_mean, group_width)) * per_channel(inv_std, group_width)
    pre_act = normed * norm_gain + norm_shift
    sigmoid_pre = jax.nn.sigmoid(pre_act)
    activated = (pre_act * sigmoid_pre).astype(bf16)
    padded = with_halo(activated, (("dom", 1),), 1)
    padded = jnp.pad(padded, ((0, 0), (0, 0), (1, 1), (0, 0)))

    def shifted(source, row_start, col_start):
        return source[
            :, row_start : row_start + row_count, col_start : col_start + col_count, :
        ].reshape(-1, chan_count)

    conv_sum = input_wide.reshape(-1, chan_count)
    for tap_index in range(9):
        row_off = tap_index // 3 - 1
        col_off = tap_index % 3 - 1
        conv_sum = conv_sum + jnp.dot(
            shifted(padded, 1 + row_off, 1 + col_off),
            conv_weight[tap_index],
            preferred_element_type=f32,
        )
    residual = conv_sum.astype(bf16)
    out_flat = out_cot.reshape(-1, chan_count)
    attended_flat = attended.reshape(-1, chan_count)
    out_grad = jnp.einsum("nc,nd->cd", attended_flat, out_flat, preferred_element_type=f32)
    d_attended = jnp.einsum("nd,cd->nc", out_flat, out_weight, preferred_element_type=f32).astype(
        bf16
    )

    def split_heads(values):
        return values.reshape(samples, -1, HEADS, head_width)

    def scores(left, right):
        return jnp.einsum("sqhd,skhd->shqk", left, right, preferred_element_type=f32) * score_scale

    q_rows = saved_q.reshape(samples, tok_count, chan_count)
    k_rows = saved_k.reshape(samples, tok_count, chan_count)
    v_rows = saved_v.reshape(samples, tok_count, chan_count)
    do_rows = d_attended.reshape(samples, tok_count, chan_count)
    q_heads = split_heads(q_rows)
    k_heads = split_heads(k_rows)
    v_heads = split_heads(v_rows)
    do_heads = split_heads(do_rows)
    row_dot = jnp.einsum(
        "sqhd,sqhd->sqh",
        split_heads(attended.reshape(samples, tok_count, chan_count)),
        do_heads,
        preferred_element_type=f32,
    )
    row_dot_t = row_dot.transpose(0, 2, 1)

    def grad_terms(query_heads, dout_heads, key_heads, value_heads, log_norm_t, dot_t):
        softmax_p = jnp.exp(scores(query_heads, key_heads) - log_norm_t[..., None])
        d_probs = jnp.einsum("sqhd,skhd->shqk", dout_heads, value_heads, preferred_element_type=f32)
        d_scores = (softmax_p * (d_probs - dot_t[..., None])).astype(bf16)
        return (softmax_p.astype(bf16), d_scores)

    row_max = jnp.full((samples, HEADS, tok_count), -jnp.inf, f32)
    row_total = jnp.zeros((samples, HEADS, tok_count), f32)
    logits = scores(q_heads, split_heads(lax.all_gather(k_rows, "dom", axis=1, tiled=True)))
    new_max = logits.max(-1)
    row_total = row_total * jnp.exp(row_max - new_max) + jnp.exp(logits - new_max[..., None]).sum(
        -1
    )
    row_max, row_total = (new_max, row_total)
    log_norm = row_max + jnp.log(row_total)
    shard_piece = (
        lax.all_gather(k_rows, "dom", axis=1, tiled=True),
        lax.all_gather(v_rows, "dom", axis=1, tiled=True),
    )
    key_heads = split_heads(shard_piece[0])
    value_heads = split_heads(shard_piece[1])
    p_half, d_scores = grad_terms(q_heads, do_heads, key_heads, value_heads, log_norm, row_dot_t)
    q_accum = jnp.einsum("shqk,skhd->sqhd", d_scores, key_heads, preferred_element_type=f32)
    stats_all = (
        lax.all_gather(log_norm.transpose(0, 2, 1), "dom", axis=1, tiled=True),
        lax.all_gather(row_dot, "dom", axis=1, tiled=True),
    )
    shard_piece = (
        lax.all_gather(q_rows, "dom", axis=1, tiled=True),
        lax.all_gather(do_rows, "dom", axis=1, tiled=True),
    )
    query_heads = split_heads(shard_piece[0])
    dout_heads = split_heads(shard_piece[1])
    norm_piece = stats_all[0].transpose(0, 2, 1)
    dot_piece = stats_all[1].transpose(0, 2, 1)
    p_half, d_scores = grad_terms(query_heads, dout_heads, k_heads, v_heads, norm_piece, dot_piece)
    k_accum = jnp.einsum("shqk,sqhd->skhd", d_scores, query_heads, preferred_element_type=f32)
    v_accum = jnp.einsum("shqk,sqhd->skhd", p_half, dout_heads, preferred_element_type=f32)
    k_accum, v_accum = (k_accum, v_accum)
    k_grad = (k_accum * score_scale).astype(bf16).reshape(samples, tok_count, chan_count)
    v_grad = v_accum.astype(bf16).reshape(samples, tok_count, chan_count)
    q_grad = (q_accum * score_scale).astype(bf16).reshape(samples, tok_count, chan_count)
    proj_grad = jnp.concatenate([q_grad, k_grad, v_grad], axis=-1).reshape(-1, 3 * chan_count)
    qkv_local = jnp.einsum("nc,nd->cd", residual, proj_grad, preferred_element_type=f32)
    d_residual = (
        out_flat.astype(f32)
        + jnp.einsum("nd,cd->nc", proj_grad, qkv_weight, preferred_element_type=f32)
    ).astype(bf16)
    d_res_map = d_residual.reshape(samples, row_count, col_count, chan_count)
    d_padded = with_halo(d_res_map, (("dom", 1),), 1)
    d_padded = jnp.pad(d_padded, ((0, 0), (0, 0), (1, 1), (0, 0)))
    conv_parts = []
    d_act = jnp.zeros((samples * tok_count, chan_count), f32)
    for tap_index in range(9):
        row_off = tap_index // 3 - 1
        col_off = tap_index % 3 - 1
        conv_parts.append(
            jnp.einsum(
                "nc,nd->cd",
                shifted(padded, 1 + row_off, 1 + col_off),
                d_residual,
                preferred_element_type=f32,
            )
        )
        d_act = d_act + jnp.einsum(
            "nd,cd->nc",
            shifted(d_padded, 1 - row_off, 1 - col_off),
            conv_weight[tap_index],
            preferred_element_type=f32,
        )
    conv_local = jnp.stack(conv_parts)
    d_pre = (
        d_act.reshape(samples, row_count, col_count, chan_count)
        * sigmoid_pre
        * (1.0 + pre_act * (1.0 - sigmoid_pre))
    )
    gain_local = (d_pre * normed).sum((0, 1, 2))
    shift_local = d_pre.sum((0, 1, 2))
    scaled = d_pre * norm_gain
    scaled_groups = scaled.reshape(samples, row_count, col_count, GROUPS, group_width)
    product_groups = (scaled * normed).reshape(samples, row_count, col_count, GROUPS, group_width)
    back_sums = lax.psum((scaled_groups.sum((1, 2, 4)), product_groups.sum((1, 2, 4))), "dom")
    first = back_sums[0] / count
    second = back_sums[1] / count
    input_grad = (
        d_res_map.astype(f32)
        + per_channel(inv_std, group_width)
        * (scaled - per_channel(first, group_width) - normed * per_channel(second, group_width))
    ).astype(bf16)
    out_grad, qkv_grad, conv_grad, gain_grad, shift_grad = lax.psum(
        (out_grad, qkv_local, conv_local, gain_local, shift_local), ("batch", "dom")
    )
    return (input_grad, conv_grad, qkv_grad, out_grad, gain_grad, shift_grad)


def solution(mesh):
    placed = (
        P("batch", "dom", None, None),
        P("batch", "dom", None, None),
        P("batch", "dom", None, None),
        P("batch", "dom", None, None),
        P("batch", "dom", None, None),
        P("batch", "dom", None, None),
        P(),
        P(),
        P(),
        P(),
        P(),
    )
    return jax.shard_map(
        body,
        mesh=mesh,
        in_specs=placed,
        out_specs=(P("batch", "dom", None, None), P(), P(), P(), P(), P()),
        check_vma=False,
    )
```

profile of v0, /device:TPU:2, one launch (start us, length us, event | category | flops | bytes accessed | tf_op | source)
XLA Modules:
  0.0 552.1 jit_solution(14365072272132767426)
XLA Ops:
  15.4 19.1 %all-gather.1 = f32[16,272,2]{1,2,0:T(2,128)S(1)} all-gather(f32[1,272,2]{1,2,0:T(2,128)S(1)} %bitcast.194), channel_id=2, replica_groups=mesh['batch'=16,'dom'=16] {'dom'}, dimensions={0}, use_global_device_ids=true | all-gather | bytes 36992 | tf_op jit(solution)/shard_map/all_gather | solution.py:135
  35.1 27.5 %all-reduce.5 = (f32[2,32]{1,0:T(2,128)S(1)}, f32[2,32]{1,0:T(2,128)S(1)}) all-reduce(f32[2,32]{1,0:T(2,128)S(1)} %reduce_sum.100, f32[2,32]{1,0:T(2,128)S(1)} %reduce_sum.81), channel_id=1, replica_groups=mesh['batch'=16,'dom'=16] {'dom'}, use_global_device_ids=true, to_apply=%region_7.8 | all-reduce | flops 128 | bytes 1024 | tf_op jit(solution)/shard_map/psum | solution.py:55
  63.5 3.8 fusion.91
  68.7 2.2 copy-done.1
  71.8 34.4 %all_gather.22 = f32[2,4352,1]{0,2,1:T(1,128)S(1)} all-gather(f32[2,272,1]{0,2,1:T(1,128)} %copy.68), channel_id=1, replica_groups=mesh['batch'=16,'dom'=16] {'dom'}, dimensions={1}, use_global_device_ids=true | all-gather | bytes 36992 | tf_op jit(solution)/shard_map/all_gather | solution.py:134
  106.9 7.5 %subtract_exponential_fusion = f32[2,4352,272]{1,2,0:T(8,128)} fusion(bf16[2,4352,256]{2,1,0:T(8,128)(2,1)} %all-gather.11.cloned.1.call-done, f32[2,4352]{1,0:T(2,128)S(1)} %copy.69, bf16[2,272,256]{2,0,1:T(2,128)(2,1)S(1)} %bitcast.185), kind=kOutput, calls=%fused_computation.1 | convolution fusion | flops 1216888832 | bytes 14239744 | tf_op jit(solution)/shard_map/sqhd,skhd->shqk/dot_general | solution.py:92
  114.3 29.6 %all-gather.13.cloned.1.call-done = bf16[2,4352,256]{2,1,0:T(8,128)(2,1)} async-done(((bf16[2,272,256]{2,1,0:T(8,128)(2,1)}), bf16[2,4352,256]{2,1,0:T(8,128)(2,1)}) %all-gather.13.cloned.1.call-update) | async-done | bytes 4456464 | tf_op jit(solution)/shard_map/all_gather | solution.py:139
  143.9 6.3 %fusion.13 = bf16[2,256,272]{1,2,0:T(8,128)(2,1)S(1)} fusion(bf16[2,4352,256]{2,1,0:T(8,128)(2,1)} %all-gather.13.cloned.1.call-done, f32[2,4352,272]{1,2,0:T(8,128)} %subtract_exponential_fusion), kind=kOutput, calls=%fused_computation.32 | convolution fusion | flops 1214660608 | bytes 14204928 | tf_op jit(solution)/shard_map/shqk,sqhd->skhd/dot_general | solution.py:147
  150.3 9.0 %fusion.12 = bf16[2,272,256]{2,1,0:T(8,128)(2,1)S(1)} fusion(bf16[2,4352,256]{2,1,0:T(8,128)(2,1)} %all-gather.11.cloned.1.call-done, f32[2,4352,272]{1,2,0:T(8,128)} %subtract_exponential_fusion, bf16[2,4352,256]{2,1,0:T(8,128)(2,1)} %all-gather.13.cloned.1.call-done, f32[2,4352]{1,0:T(2,128)S(1)} %bitcast.189, bf16[2,272,256]{2,0,1:T(2,128)(2,1)S(1)} %bitcast.187), kind=kOutput, calls=%fused_computation.31 | convolution fusion | flops 2431688704 | bytes 18974720 | tf_op jit(solution)/shard_map/shqk,sqhd->skhd/dot_general | solution.py:146
  159.3 26.3 %all-gather.9.cloned.1.call-done = bf16[2,4352,256]{2,0,1:T(2,128)(2,1)} async-done(((bf16[2,272,256]{2,0,1:T(2,128)(2,1)}), bf16[2,4352,256]{2,0,1:T(2,128)(2,1)}) %all-gather.9.cloned.1.call-update) | async-done | bytes 4456464 | tf_op jit(solution)/shard_map/all_gather | solution.py:127
  185.6 10.2 %fusion.18 = bf16[2,272,256]{2,1,0:T(8,128)(2,1)S(1)} fusion(bf16[2,4352,256]{2,1,0:T(8,128)(2,1)} %all-gather.7.cloned.1.call-done, f32[2,272,4352]{2,1,0:T(8,128)} %copy-done.1, bf16[2,272,256]{2,1,0:T(8,128)(2,1)S(1)} %bitcast.183, f32[2,272]{1,0:T(2,128)S(1)} %copy.80, f32[2,272]{1,0:T(2,128)S(1)} %log_add_fusion, ...), kind=kOutput, calls=%fused_computation.36 | convolution fusion | flops 2434056192 | bytes 18944256 | tf_op jit(solution)/shard_map/shqk,skhd->sqhd/dot_general | solution.py:132
  197.0 2.1 collective-permute-start
  199.2 5.8 %collective-permute-start.1 = (bf16[2,1,68,256]{3,2,1,0:T(8,128)(2,1)S(1)}, bf16[2,1,68,256]{3,2,1,0:T(8,128)(2,1)S(1)}, u32[]{:S(2)}, u32[]{:S(2)}) collective-permute-start(bf16[2,1,68,256]{3,2,1,0:T(8,128)(2,1)S(1)} %get-tuple-element.59), channel_id=1, source_target_pairs={{1,0},{2,1},{3,2},{4,3},{5,4},{6,5},{7,6},{8,7},{9,8},{10,9},{11,1... | collective-permute-start | bytes 208904 | tf_op jit(solution)/shard_map/ppermute | solution.py:21
  229.4 5.8 %collective-permute-start.3 = (bf16[2,1,68,256]{3,2,1,0:T(8,128)(2,1)S(1)}, bf16[2,1,68,256]{3,2,1,0:T(8,128)(2,1)S(1)}, u32[]{:S(2)}, u32[]{:S(2)}) collective-permute-start(bf16[2,1,68,256]{3,2,1,0:T(8,128)(2,1)S(1)} %get-tuple-element.55), channel_id=1, source_target_pairs={{1,0},{2,1},{3,2},{4,3},{5,4},{6,5},{7,6},{8,7},{9,8},{10,9},{11,1... | collective-permute-start | bytes 208904 | tf_op jit(solution)/shard_map/ppermute | solution.py:21
  235.2 2.0 convolution_bitcast_fusion
  242.9 2.0 fusion.30
  244.8 2.2 convolution_add_fusion.7
  256.4 2.0 fusion.29
  258.3 2.0 fusion.28
  269.3 3.2 fusion.21
  272.9 29.0 %all-reduce.4 = (f32[2,32]{1,0:T(2,128)S(1)}, f32[2,32]{1,0:T(2,128)S(1)}) all-reduce(f32[2,32]{1,0:T(2,128)S(1)} %reduce_sum.106, f32[2,32]{1,0:T(2,128)S(1)} %reduce_sum.103), channel_id=1, replica_groups=mesh['batch'=16,'dom'=16] {'dom'}, use_global_device_ids=true, to_apply=%region_13.14 | all-reduce | flops 128 | bytes 1024 | tf_op jit(solution)/shard_map/psum | solution.py:191
  303.3 74.3 %all-reduce.2 = (f32[256]{0:T(256)}, f32[256]{0:T(256)}) all-reduce(f32[256]{0:T(256)S(1)} %get-tuple-element.24, f32[256]{0:T(256)S(1)} %get-tuple-element.27), channel_id=1, replica_groups=mesh['batch'=16,'dom'=16] {'batch','dom'}, use_global_device_ids=true, to_apply=%region_18.19 | all-reduce | flops 512 | bytes 4096 | tf_op jit(solution)/shard_map/psum | solution.py:199
  377.7 163.0 %all-reduce.8.cloned.1.call-done = (f32[9,256,256]{2,1,0:T(8,128)}, f32[256,768]{1,0:T(8,128)}, f32[256,256]{1,0:T(8,128)}) async-done(((f32[9,256,256]{2,1,0:T(8,128)}, f32[256,768]{1,0:T(8,128)}, f32[256,256]{1,0:T(8,128)}), (f32[9,256,256]{2,1,0:T(8,128)}, f32[256,768]{1,0:T(8,128)}, f32[256,256]{1,0:T(8,128)})) %all-reduce.8.cloned.1.call-update) | async-done | bytes 3407888 | tf_op jit(solution)/shard_map/psum | solution.py:199
  540.7 3.3 copy.124
  (165 shorter events, 65.1 us)
Async XLA Ops:
  7.2 189.4 %copy-start = (bf16[256,768]{1,0:T(8,128)(2,1)S(1)}, bf16[256,768]{1,0:T(8,128)(2,1)}, u32[]{:S(2)}) copy-start(bf16[256,768]{1,0:T(8,128)(2,1)} %param.18) | copy-start | bytes 1179652
  7.2 4.1 copy-start.19
  7.2 4.2 copy-start.23
  7.2 5.3 copy-start.18
  7.2 56.2 %all-gather.7.cloned.1.call-start = ((), (), s32[]{:S(2)}) async-start(), calls=%async_computation | async-start | bytes 4734976 | tf_op jit(solution)/shard_map/all_gather | solution.py:126
  9.3 97.6 %all-gather.11.cloned.1.call-start = ((), (), s32[]{:S(2)}) async-start(), calls=%async_computation.2 | async-start | bytes 4734976 | tf_op jit(solution)/shard_map/all_gather | solution.py:138
  11.3 132.7 %all-gather.13.cloned.1.call-start = ((), (), s32[]{:S(2)}) async-start(), calls=%async_computation.3 | async-start | bytes 4734976 | tf_op jit(solution)/shard_map/all_gather | solution.py:139
  11.4 23.2 %copy-start.2 = (bf16[2,4,68,256]{3,1,2,0:T(4,128)(2,1)S(1)}, bf16[2,4,68,256]{3,1,2,0:T(4,128)(2,1)}, u32[]{:S(2)}) copy-start(bf16[2,4,68,256]{3,1,2,0:T(4,128)(2,1)} %param.11) | copy-start | bytes 835588
  12.5 173.2 %all-gather.9.cloned.1.call-start = ((), (), s32[]{:S(2)}) async-start(), calls=%async_computation.1 | async-start | bytes 4734976 | tf_op jit(solution)/shard_map/all_gather | solution.py:127
  13.5 527.2 %all-reduce.8.cloned.1.call-start = ((), (), s32[]{:S(2)}) async-start(), calls=%async_computation.4 | async-start | bytes 6815744 | tf_op jit(solution)/shard_map/psum | solution.py:199
  114.3 36.0 %copy-start.8 = (bf16[2,4,68,256]{3,0,2,1:T(2,128)(2,1)S(1)}, bf16[2,4,68,256]{3,0,2,1:T(2,128)(2,1)}, u32[]{:S(2)}) copy-start(bf16[2,4,68,256]{3,0,2,1:T(2,128)(2,1)} %copy.63) | copy-start | bytes 835588
  150.3 45.6 %copy-start.17 = (bf16[2,256,272]{1,2,0:T(8,128)(2,1)}, bf16[2,256,272]{1,2,0:T(8,128)(2,1)S(1)}, u32[]{:S(2)}) copy-start(bf16[2,256,272]{1,2,0:T(8,128)(2,1)S(1)} %fusion.13) | copy-start | bytes 835588
  150.3 35.4 %copy-start.4 = (bf16[544,256]{1,0:T(8,128)(2,1)S(1)}, bf16[544,256]{1,0:T(8,128)(2,1)}, u32[]{:S(2)}) copy-start(bf16[544,256]{1,0:T(8,128)(2,1)} %convolution_convert_fusion) | copy-start | bytes 835588
  159.3 36.5 %copy-start.21 = (bf16[2,272,256]{2,1,0:T(8,128)(2,1)}, bf16[2,272,256]{2,1,0:T(8,128)(2,1)S(1)}, u32[]{:S(2)}) copy-start(bf16[2,272,256]{2,1,0:T(8,128)(2,1)S(1)} %fusion.12) | copy-start | bytes 835588
  197.0 8.3 %collective-permute-start = (bf16[2,1,68,256]{3,2,1,0:T(8,128)(2,1)S(1)}, bf16[2,1,68,256]{3,2,1,0:T(8,128)(2,1)S(1)}, u32[]{:S(2)}, u32[]{:S(2)}) collective-permute-start(bf16[2,1,68,256]{3,2,1,0:T(8,128)(2,1)S(1)} %get-tuple-element.58), channel_id=1, source_target_pairs={{0,1},{1,2},{2,3},{3,4},{4,5},{5,6},{6,7},{7,8},{8,9},{9,10},{10,1... | collective-permute-start | bytes 208904 | tf_op jit(solution)/shard_map/ppermute | solution.py:19
  199.2 7.5 %collective-permute-start.1 = (bf16[2,1,68,256]{3,2,1,0:T(8,128)(2,1)S(1)}, bf16[2,1,68,256]{3,2,1,0:T(8,128)(2,1)S(1)}, u32[]{:S(2)}, u32[]{:S(2)}) collective-permute-start(bf16[2,1,68,256]{3,2,1,0:T(8,128)(2,1)S(1)} %get-tuple-element.59), channel_id=1, source_target_pairs={{1,0},{2,1},{3,2},{4,3},{5,4},{6,5},{7,6},{8,7},{9,8},{10,9},{11,1... | collective-permute-start | bytes 208904 | tf_op jit(solution)/shard_map/ppermute | solution.py:21
  227.5 11.8 %collective-permute-start.2 = (bf16[2,1,68,256]{3,2,1,0:T(8,128)(2,1)S(1)}, bf16[2,1,68,256]{3,2,1,0:T(8,128)(2,1)S(1)}, u32[]{:S(2)}, u32[]{:S(2)}) collective-permute-start(bf16[2,1,68,256]{3,2,1,0:T(8,128)(2,1)S(1)} %get-tuple-element.54), channel_id=1, source_target_pairs={{0,1},{1,2},{2,3},{3,4},{4,5},{5,6},{6,7},{7,8},{8,9},{9,10},{10,1... | collective-permute-start | bytes 208904 | tf_op jit(solution)/shard_map/ppermute | solution.py:19
  229.4 9.9 %collective-permute-start.3 = (bf16[2,1,68,256]{3,2,1,0:T(8,128)(2,1)S(1)}, bf16[2,1,68,256]{3,2,1,0:T(8,128)(2,1)S(1)}, u32[]{:S(2)}, u32[]{:S(2)}) collective-permute-start(bf16[2,1,68,256]{3,2,1,0:T(8,128)(2,1)S(1)} %get-tuple-element.55), channel_id=1, source_target_pairs={{1,0},{2,1},{3,2},{4,3},{5,4},{6,5},{7,6},{8,7},{9,8},{10,9},{11,1... | collective-permute-start | bytes 208904 | tf_op jit(solution)/shard_map/ppermute | solution.py:21
  248.0 4.5 copy-start.7
  255.3 5.0 copy-start.10
  255.3 5.0 copy-start.11
  255.3 6.2 %copy-start.6 = (bf16[544,256]{1,0:T(8,128)(2,1)S(1)}, bf16[544,256]{1,0:T(8,128)(2,1)}, u32[]{:S(2)}) copy-start(bf16[544,256]{1,0:T(8,128)(2,1)} %reshape.277) | copy-start | bytes 835588
  272.5 29.8 %copy-start.9 = (f32[2,4,68,256]{3,2,1,0:T(8,128)S(1)}, f32[2,4,68,256]{3,2,1,0:T(8,128)}, u32[]{:S(2)}) copy-start(f32[2,4,68,256]{3,2,1,0:T(8,128)} %get-tuple-element.39) | copy-start | bytes 1671172
  540.7 4.2 copy-start.22
  (12 other events, 33.9 us)
Sparse Core Ops, SparseCore 0:
  9.8 42.8 all-gather.6
  55.1 46.8 all-gather.10
  104.3 39.5 all-gather.12
  145.6 39.9 all-gather.8
  272.7 267.9 all-reduce.7
where the time goes:
time: 553 us; the launch traced here: 552 us
  waiting for transfers between devices  220 us (40%)
  blocking collectives  184 us (33%)
  matrix products  69.6 us (13%)
  local copies, waits for them, and re-layouts  39.9 us (7%)
  starting transfers between devices  15.8 us (3%)
  between operations  14.4 us (3%)
  other arithmetic  7.61 us (1%)
    psum x1, waiting for transfers between devices, body(): lax.psum((out_grad, qkv_local, conv_local, gain_local, shift_local), ('ba...  163 us
    psum x1, blocking collectives, body(): lax.psum((out_grad, qkv_local, conv_local, gain_local, shift_local), ('ba...  74.3 us
    all_gather x1, blocking collectives, body(): lax.all_gather(log_norm.transpose(0, 2, 1), 'dom', axis=1, tiled=True)  34.4 us
    all_gather x1, waiting for transfers between devices, body(): lax.all_gather(do_rows, 'dom', axis=1, tiled=True)  29.6 us
    psum x1, blocking collectives, body(): lax.psum((scaled_groups.sum((1, 2, 4)), product_groups.sum((1, 2, 4))), '...  29 us
    psum x1, blocking collectives, body(): lax.psum((grouped.sum((1, 2, 4)), (grouped * grouped).sum((1, 2, 4))), 'd...  27.5 us
    all_gather x1, waiting for transfers between devices, body(): lax.all_gather(v_rows, 'dom', axis=1, tiled=True)  26.3 us
    all_gather x1, blocking collectives, body(): lax.all_gather(row_dot, 'dom', axis=1, tiled=True)  19.1 us
  transfers between devices with their start and end apart: 9, of which 4 were waited for; matrix products, arithmetic and copies ran while one was open for 8% of the time, Pallas kernels for 0%

commit v1 on v0

--- a/solution.py
+++ b/solution.py
@@ -124,7 +124,9 @@
     log_norm = row_max + jnp.log(row_total)
     shard_piece = (
         lax.all_gather(k_rows, "dom", axis=1, tiled=True),
-        lax.all_gather(v_rows, "dom", axis=1, tiled=True),
+        jnp.concatenate(
+            lax.all_to_all(jnp.stack([v_rows] * lax.axis_size("dom")), "dom", 0, 0), axis=1
+        ),
     )
     key_heads = split_heads(shard_piece[0])
     value_heads = split_heads(shard_piece[1])

time: 553 us -> 583 us (1.054)
  blocking collectives: 184 us -> 260 us
  waiting for transfers between devices: 220 us -> 163 us
  starting transfers between devices: 15.8 us -> 22.5 us
  local copies, waits for them, and re-layouts: 39.9 us -> 45.8 us
    all_gather x1, blocking collectives: 19.1 us -> 87.3 us  [body(): lax.all_gather(row_dot, 'dom', axis=1, tiled=True)]
    all_gather x1, waiting for transfers between devices: 29.6 us -> 0.01 us  [body(): lax.all_gather(do_rows, 'dom', axis=1, tiled=True)]
    all_gather x1 -> x0, waiting for transfers between devices: 26.3 us -> none  [body(): lax.all_gather(v_rows, 'dom', axis=1, tiled=True)]
    all_to_all x0 -> x1, starting transfers between devices: none -> 6.72 us  [body(): lax.all_to_all(jnp.stack([v_rows] * lax.axis_size('dom')), 'dom', 0, 0)]
    unnamed x64 -> x70, local copies, waits for them, and re-layouts: 12.5 us -> 11.2 us
  transfers between devices with their start and end apart: 9 -> 9, of which waited for: 4 -> 2; matrix products, arithmetic and copies ran while one was open for 8% -> 6% of each run, Pallas kernels for 0% -> 0%
where the time goes in v1:
time: 583 us; the launch traced here: 582 us
  blocking collectives  260 us (45%)
  waiting for transfers between devices  163 us (28%)
  matrix products  69.5 us (12%)
  local copies, waits for them, and re-layouts  45.8 us (8%)
  starting transfers between devices  22.5 us (4%)
  between operations  14.5 us (2%)
  other arithmetic  6.67 us (1%)
    psum x1, waiting for transfers between devices, body(): lax.psum((out_grad, qkv_local, conv_local, gain_local, shift_local), ('ba...  162 us
    all_gather x1, blocking collectives, body(): lax.all_gather(row_dot, 'dom', axis=1, tiled=True)  87.3 us
    psum x1, blocking collectives, body(): lax.psum((out_grad, qkv_local, conv_local, gain_local, shift_local), ('ba...  79 us
    all_gather x1, blocking collectives, body(): lax.all_gather(log_norm.transpose(0, 2, 1), 'dom', axis=1, tiled=True)  35.2 us
    psum x1, blocking collectives, body(): lax.psum((grouped.sum((1, 2, 4)), (grouped * grouped).sum((1, 2, 4))), 'd...  29.7 us
    psum x1, blocking collectives, body(): lax.psum((scaled_groups.sum((1, 2, 4)), product_groups.sum((1, 2, 4))), '...  28.9 us
    reshape x17, local copies, waits for them, and re-layouts, shifted(): return source[:, row_start:row_start + row_count, col_start:col_start + c...  18 us
    dot_general x9, matrix products, body(): jnp.einsum('nc,nd->cd', shifted(padded, 1 + row_off, 1 + col_off), d_resi...  11.9 us
  transfers between devices with their start and end apart: 9, of which 2 were waited for; matrix products, arithmetic and copies ran while one was open for 6% of the time, Pallas kernels for 0%

profile of v1, /device:TPU:2, one launch (start us, length us, event | category | flops | bytes accessed | tf_op | source)
XLA Modules:
  0.0 582.2 jit_solution(14340100272314735308)
XLA Ops:
  12.8 2.5 stack.33
  15.3 6.7 %all-to-all-start = ((bf16[16,2,272,256]{3,2,1,0:T(8,128)(2,1)}), bf16[16,2,272,256]{3,2,1,0:T(8,128)(2,1)}, u32[]{:S(2)}, u32[]{:S(2)}) async-start(bf16[16,2,272,256]{3,2,1,0:T(8,128)(2,1)} %stack.33), calls=%async_computation | async-start | bytes 8912896 | tf_op jit(solution)/shard_map/all_to_all | solution.py:128
  23.0 87.3 %all-gather.1 = f32[16,272,2]{1,2,0:T(2,128)S(1)} all-gather(f32[1,272,2]{1,2,0:T(2,128)S(1)} %bitcast.199), channel_id=2, replica_groups=mesh['batch'=16,'dom'=16] {'dom'}, dimensions={0}, use_global_device_ids=true | all-gather | bytes 36992 | tf_op jit(solution)/shard_map/all_gather | solution.py:137
  110.9 29.7 %all-reduce.5 = (f32[2,32]{1,0:T(2,128)S(1)}, f32[2,32]{1,0:T(2,128)S(1)}) all-reduce(f32[2,32]{1,0:T(2,128)S(1)} %reduce_sum.100, f32[2,32]{1,0:T(2,128)S(1)} %reduce_sum.81), channel_id=1, replica_groups=mesh['batch'=16,'dom'=16] {'dom'}, use_global_device_ids=true, to_apply=%region_7.8 | all-reduce | flops 128 | bytes 1024 | tf_op jit(solution)/shard_map/psum | solution.py:55
  141.4 4.6 copy.67
  146.1 3.8 fusion.82
  151.3 2.2 copy-done.1
  154.4 35.2 %all_gather.18 = f32[2,4352,1]{0,2,1:T(1,128)S(1)} all-gather(f32[2,272,1]{0,2,1:T(1,128)} %copy.71), channel_id=1, replica_groups=mesh['batch'=16,'dom'=16] {'dom'}, dimensions={1}, use_global_device_ids=true | all-gather | bytes 36992 | tf_op jit(solution)/shard_map/all_gather | solution.py:136
  190.2 7.5 %subtract_exponential_fusion = f32[2,4352,272]{1,2,0:T(8,128)} fusion(bf16[2,4352,256]{2,1,0:T(8,128)(2,1)} %all-gather.8.cloned.1.call-done, f32[2,4352]{1,0:T(2,128)S(1)} %copy.72, bf16[2,272,256]{2,0,1:T(2,128)(2,1)S(1)} %bitcast.190), kind=kOutput, calls=%fused_computation.1 | convolution fusion | flops 1216888832 | bytes 14239744 | tf_op jit(solution)/shard_map/sqhd,skhd->shqk/dot_general | solution.py:92
  197.8 6.6 %fusion.7 = bf16[2,256,272]{1,2,0:T(8,128)(2,1)S(1)} fusion(bf16[2,4352,256]{2,1,0:T(8,128)(2,1)} %all-gather.10.cloned.1.call-done, f32[2,4352,272]{1,2,0:T(8,128)} %subtract_exponential_fusion), kind=kOutput, calls=%fused_computation.31 | convolution fusion | flops 1214660608 | bytes 14204928 | tf_op jit(solution)/shard_map/shqk,sqhd->skhd/dot_general | solution.py:149
  204.4 9.0 %fusion.6 = bf16[2,272,256]{2,1,0:T(8,128)(2,1)S(1)} fusion(bf16[2,4352,256]{2,1,0:T(8,128)(2,1)} %all-gather.8.cloned.1.call-done, f32[2,4352,272]{1,2,0:T(8,128)} %subtract_exponential_fusion, bf16[2,4352,256]{2,1,0:T(8,128)(2,1)} %all-gather.10.cloned.1.call-done, f32[2,4352]{1,0:T(2,128)S(1)} %bitcast.194, bf16[2,272,256]{2,0,1:T(2,128)(2,1)S(1)} %bitcast.192), kind=kOutput, calls=%fused_computation.30 | convolution fusion | flops 2431688704 | bytes 18974720 | tf_op jit(solution)/shard_map/shqk,sqhd->skhd/dot_general | solution.py:148
  213.4 9.8 %fusion.5 = bf16[2,272,256]{2,1,0:T(8,128)(2,1)S(1)} fusion(bf16[2,4352,256]{2,1,0:T(8,128)(2,1)} %all-gather.6.cloned.1.call-done, f32[2,272,4352]{2,1,0:T(8,128)} %copy-done.1, bf16[2,272,256]{2,1,0:T(8,128)(2,1)S(1)} %bitcast.188, bf16[2,4352,256]{2,1,0:T(8,128)(2,1)} %bitcast.183, f32[2,272]{1,0:T(2,128)S(1)} %copy.83, f32[2,272]{1,0:T(2,128)S(1)} %log_add_fusion), kind=kOutput, calls=%fused_computation.29 | convolution fusion | flops 2434056192 | bytes 18944256 | tf_op jit(solution)/shard_map/shqk,skhd->sqhd/dot_general | solution.py:134
  223.9 2.2 collective-permute-start
  226.1 5.4 collective-permute-start.1
  254.3 2.1 collective-permute-start.2
  256.5 5.8 collective-permute-start.3
  262.3 2.0 convolution_bitcast_fusion
  269.9 2.0 fusion.21
  271.9 2.2 convolution_add_fusion.7
  296.4 3.2 fusion.12
  300.0 28.9 %all-reduce.4 = (f32[2,32]{1,0:T(2,128)S(1)}, f32[2,32]{1,0:T(2,128)S(1)}) all-reduce(f32[2,32]{1,0:T(2,128)S(1)} %reduce_sum.106, f32[2,32]{1,0:T(2,128)S(1)} %reduce_sum.103), channel_id=1, replica_groups=mesh['batch'=16,'dom'=16] {'dom'}, use_global_device_ids=true, to_apply=%region_13.14 | all-reduce | flops 128 | bytes 1024 | tf_op jit(solution)/shard_map/psum | solution.py:193
  330.3 79.0 %all-reduce.2 = (f32[256]{0:T(256)}, f32[256]{0:T(256)}) all-reduce(f32[256]{0:T(256)S(1)} %get-tuple-element.24, f32[256]{0:T(256)S(1)} %get-tuple-element.27), channel_id=1, replica_groups=mesh['batch'=16,'dom'=16] {'batch','dom'}, use_global_device_ids=true, to_apply=%region_18.19 | all-reduce | flops 512 | bytes 4096 | tf_op jit(solution)/shard_map/psum | solution.py:201
  409.2 161.5 %all-reduce.8.cloned.1.call-done = (f32[9,256,256]{2,1,0:T(8,128)}, f32[256,768]{1,0:T(8,128)}, f32[256,256]{1,0:T(8,128)}) async-done(((f32[9,256,256]{2,1,0:T(8,128)}, f32[256,768]{1,0:T(8,128)}, f32[256,256]{1,0:T(8,128)}), (f32[9,256,256]{2,1,0:T(8,128)}, f32[256,768]{1,0:T(8,128)}, f32[256,256]{1,0:T(8,128)})) %all-reduce.8.cloned.1.call-update) | async-done | bytes 3407888 | tf_op jit(solution)/shard_map/psum | solution.py:201
  570.8 3.3 copy.119
  (173 shorter events, 65.1 us)
Async XLA Ops:
  7.2 216.1 %copy-start = (bf16[256,768]{1,0:T(8,128)(2,1)S(1)}, bf16[256,768]{1,0:T(8,128)(2,1)}, u32[]{:S(2)}) copy-start(bf16[256,768]{1,0:T(8,128)(2,1)} %param.18) | copy-start | bytes 1179652
  7.2 4.3 copy-start.26
  7.2 5.3 copy-start.21
  7.2 138.8 %all-gather.6.cloned.1.call-start = ((), (), s32[]{:S(2)}) async-start(), calls=%async_computation.1 | async-start | bytes 4734976 | tf_op jit(solution)/shard_map/all_gather | solution.py:126
  9.3 180.9 %all-gather.8.cloned.1.call-start = ((), (), s32[]{:S(2)}) async-start(), calls=%async_computation.2 | async-start | bytes 4734976 | tf_op jit(solution)/shard_map/all_gather | solution.py:140
  11.3 186.5 %all-gather.10.cloned.1.call-start = ((), (), s32[]{:S(2)}) async-start(), calls=%async_computation.3 | async-start | bytes 4734976 | tf_op jit(solution)/shard_map/all_gather | solution.py:141
  15.3 6.8 %copy-start.4 = (bf16[544,256]{1,0:T(8,128)(2,1)S(1)}, bf16[544,256]{1,0:T(8,128)(2,1)}, u32[]{:S(2)}) copy-start(bf16[544,256]{1,0:T(8,128)(2,1)} %convolution_convert_fusion) | copy-start | bytes 835588
  15.3 6.8 %copy-start.23 = (bf16[2,4,68,256]{3,1,2,0:T(4,128)(2,1)S(1)}, bf16[2,4,68,256]{3,1,2,0:T(4,128)(2,1)}, u32[]{:S(2)}) copy-start(bf16[2,4,68,256]{3,1,2,0:T(4,128)(2,1)} %param.15) | copy-start | bytes 835588
  15.3 126.1 %all-to-all-start = ((bf16[16,2,272,256]{3,2,1,0:T(8,128)(2,1)}), bf16[16,2,272,256]{3,2,1,0:T(8,128)(2,1)}, u32[]{:S(2)}, u32[]{:S(2)}) async-start(bf16[16,2,272,256]{3,2,1,0:T(8,128)(2,1)} %stack.33), calls=%async_computation | async-start | bytes 8912896 | tf_op jit(solution)/shard_map/all_to_all | solution.py:128
  22.0 88.4 %copy-start.2 = (bf16[2,4,68,256]{3,1,2,0:T(4,128)(2,1)S(1)}, bf16[2,4,68,256]{3,1,2,0:T(4,128)(2,1)}, u32[]{:S(2)}) copy-start(bf16[2,4,68,256]{3,1,2,0:T(4,128)(2,1)} %param.11) | copy-start | bytes 835588
  22.0 548.7 %all-reduce.8.cloned.1.call-start = ((), (), s32[]{:S(2)}) async-start(), calls=%async_computation.4 | async-start | bytes 6815744 | tf_op jit(solution)/shard_map/psum | solution.py:201
  197.8 6.6 %copy-start.9 = (bf16[2,4,68,256]{3,0,2,1:T(2,128)(2,1)S(1)}, bf16[2,4,68,256]{3,0,2,1:T(2,128)(2,1)}, u32[]{:S(2)}) copy-start(bf16[2,4,68,256]{3,0,2,1:T(2,128)(2,1)} %copy-done.8) | copy-start | bytes 835588
  204.4 18.9 %copy-start.20 = (bf16[2,256,272]{1,2,0:T(8,128)(2,1)}, bf16[2,256,272]{1,2,0:T(8,128)(2,1)S(1)}, u32[]{:S(2)}) copy-start(bf16[2,256,272]{1,2,0:T(8,128)(2,1)S(1)} %fusion.7) | copy-start | bytes 835588
  213.4 9.9 %copy-start.24 = (bf16[2,272,256]{2,1,0:T(8,128)(2,1)}, bf16[2,272,256]{2,1,0:T(8,128)(2,1)S(1)}, u32[]{:S(2)}) copy-start(bf16[2,272,256]{2,1,0:T(8,128)(2,1)S(1)} %fusion.6) | copy-start | bytes 835588
  213.4 9.9 %copy-start.14 = (bf16[544,256]{1,0:T(8,128)(2,1)S(1)}, bf16[544,256]{1,0:T(8,128)(2,1)}, u32[]{:S(2)}) copy-start(bf16[544,256]{1,0:T(8,128)(2,1)} %copy-done.13) | copy-start | bytes 835588
  223.9 8.0 %collective-permute-start = (bf16[2,1,68,256]{3,2,1,0:T(8,128)(2,1)S(1)}, bf16[2,1,68,256]{3,2,1,0:T(8,128)(2,1)S(1)}, u32[]{:S(2)}, u32[]{:S(2)}) collective-permute-start(bf16[2,1,68,256]{3,2,1,0:T(8,128)(2,1)S(1)} %get-tuple-element.58), channel_id=1, source_target_pairs={{0,1},{1,2},{2,3},{3,4},{4,5},{5,6},{6,7},{7,8},{8,9},{9,10},{10,1... | collective-permute-start | bytes 208904 | tf_op jit(solution)/shard_map/ppermute | solution.py:19
  226.1 7.4 %collective-permute-start.1 = (bf16[2,1,68,256]{3,2,1,0:T(8,128)(2,1)S(1)}, bf16[2,1,68,256]{3,2,1,0:T(8,128)(2,1)S(1)}, u32[]{:S(2)}, u32[]{:S(2)}) collective-permute-start(bf16[2,1,68,256]{3,2,1,0:T(8,128)(2,1)S(1)} %get-tuple-element.59), channel_id=1, source_target_pairs={{1,0},{2,1},{3,2},{4,3},{5,4},{6,5},{7,6},{8,7},{9,8},{10,9},{11,1... | collective-permute-start | bytes 208904 | tf_op jit(solution)/shard_map/ppermute | solution.py:21
  254.3 12.0 %collective-permute-start.2 = (bf16[2,1,68,256]{3,2,1,0:T(8,128)(2,1)S(1)}, bf16[2,1,68,256]{3,2,1,0:T(8,128)(2,1)S(1)}, u32[]{:S(2)}, u32[]{:S(2)}) collective-permute-start(bf16[2,1,68,256]{3,2,1,0:T(8,128)(2,1)S(1)} %get-tuple-element.54), channel_id=1, source_target_pairs={{0,1},{1,2},{2,3},{3,4},{4,5},{5,6},{6,7},{7,8},{8,9},{9,10},{10,1... | collective-permute-start | bytes 208904 | tf_op jit(solution)/shard_map/ppermute | solution.py:19
  256.5 9.9 %collective-permute-start.3 = (bf16[2,1,68,256]{3,2,1,0:T(8,128)(2,1)S(1)}, bf16[2,1,68,256]{3,2,1,0:T(8,128)(2,1)S(1)}, u32[]{:S(2)}, u32[]{:S(2)}) collective-permute-start(bf16[2,1,68,256]{3,2,1,0:T(8,128)(2,1)S(1)} %get-tuple-element.55), channel_id=1, source_target_pairs={{1,0},{2,1},{3,2},{4,3},{5,4},{6,5},{7,6},{8,7},{9,8},{10,9},{11,1... | collective-permute-start | bytes 208904 | tf_op jit(solution)/shard_map/ppermute | solution.py:21
  275.1 4.5 copy-start.7
  282.4 5.0 copy-start.11
  282.4 5.0 copy-start.12
  282.4 6.1 %copy-start.6 = (bf16[544,256]{1,0:T(8,128)(2,1)S(1)}, bf16[544,256]{1,0:T(8,128)(2,1)}, u32[]{:S(2)}) copy-start(bf16[544,256]{1,0:T(8,128)(2,1)} %reshape.281) | copy-start | bytes 835588
  299.6 29.7 %copy-start.10 = (f32[2,4,68,256]{3,2,1,0:T(8,128)S(1)}, f32[2,4,68,256]{3,2,1,0:T(8,128)}, u32[]{:S(2)}) copy-start(f32[2,4,68,256]{3,2,1,0:T(8,128)} %get-tuple-element.39) | copy-start | bytes 1671172
  (15 other events, 42.1 us)
Sparse Core Ops, SparseCore 0:
  9.8 87.8 all-gather.5
  99.5 45.5 all-gather.7
  147.5 45.7 all-gather.9
  299.7 271.0 all-reduce.7
